TPU v7x, 128 devices: a whole 4x4x4 slice. The times are simulated.
128 devices in a mesh: wave: 16 (over y, z_lo, core), pole: 8 (over x, z_hi).
Axes of the slice: x: 4, y: 4, z: 4 (z_hi: 2, z_lo: 2; z = z_hi * 2 + z_lo), core: 2. Of those that a mesh axis runs over, the one named last changes fastest.
Arguments:
- grid: float32 [6, 256, 3072], P(None, None, 'wave'), may hold values from -6 to 6
- legendre: bfloat16 [256, 2, 1536, 1024], P('wave', None, None, 'pole'), may hold values from -0.15625 to 0.15625
- wave_table: int32 [256], replicated, may hold values from 0 to 255, each once
- pole_table: float32 [4, 64], replicated, may hold values from -1.5 to 2.5, as said below
- pole_index: int32 [32], replicated, may hold values from 0 to 63
Outputs:
- next_state: float32 [6, 2, 256, 1024], P(None, None, 'wave', 'pole')
Inputs may be any that keep to these rules, and one draw needn't show every extreme that they name: Slot s holds zonal wavenumber wave_table[s], every wavenumber of 0 to 255 once; row s of legendre belongs to it. `pole_table`: shift real parts lie in 1.5 to 2.5, shift imaginary parts in -1.5 to 1.5, weights in -1.2 to 1.2.
All inputs are finite; a program needn't handle non-finite values.
Results may differ from a plain program's by a relative error of at most 0.0003.
Values sent between devices are 32-bit elements; how exact they have to be, the bound alone decides.
No kernel may reach another device: no remote copies, remote signals or barrier semaphores. Data moves between devices by JAX's collectives and lax.ppermute only.
A program may use at most 128 MiB of HBM per device.

v0:
```python
import jax
import jax.numpy as jnp
from jax import lax
from jax.sharding import PartitionSpec as P

SWEEPS = 8
coriolis_step = 1.2
gravity_step = 0.0008


def split_high(values):
    upper_part = values.astype(jnp.bfloat16)
    kept = lax.optimization_barrier(upper_part)
    lower_part = (values - kept.astype(jnp.float32)).astype(jnp.bfloat16)
    return (upper_part, lower_part)


def coefficients(wavenum, count):
    index = jnp.arange(count, dtype=jnp.int32).astype(jnp.float32)
    parity = jnp.arange(2, dtype=jnp.int32).astype(jnp.float32)
    order = (2.0 * index[None, :] + parity[:, None])[:, None, :]
    wave = wavenum[None, :, None]
    degree = wave + order
    product = degree * (degree + 1.0)
    rossby = coriolis_step * wave / jnp.maximum(product, 2.0)
    gravity = gravity_step * jnp.sqrt(product)
    e_lo = jnp.sqrt(order * (2.0 * wave + order) / jnp.maximum(4.0 * degree * degree - 1.0, 1.0))
    after = order + 1.0
    upper_deg = degree + 1.0
    e_hi = jnp.sqrt(
        after * (2.0 * wave + after) / jnp.maximum(4.0 * upper_deg * upper_deg - 1.0, 1.0)
    )
    return (e_lo, e_hi, rossby, gravity)


def cmul(are, aim, bre, bim):
    return (are * bre - aim * bim, are * bim + aim * bre)


def zero_extend(field):
    return jnp.pad(field, ((0, 0), (0, 0), (0, 0), (0, 0), (1, 1)))


def solve(spectra, coef, shifts, extend):
    e_lo, e_hi, rossby, gravity = coef
    count = spectra.shape[3]
    shift_re = shifts[:, 0][:, None, None, None]
    shift_im = shifts[:, 1][:, None, None, None]
    weight_re = shifts[:, 2][:, None, None, None]
    weight_im = shifts[:, 3][:, None, None, None]
    z0r, z0i = (spectra[0][None], spectra[1][None])
    d0r, d0i = (spectra[2][None], spectra[3][None])
    h0r, h0i = (spectra[4][None], spectra[5][None])
    b_re = shift_re + 0.0 * rossby[None]
    b_im = shift_im + rossby[None]
    b_mag = b_re * b_re + b_im * b_im
    inv_re, inv_im = (b_re / b_mag, -b_im / b_mag)
    det_re, det_im = cmul(b_re, b_im, shift_re, shift_im)
    det_re = det_re + gravity[None] * gravity[None]
    det_mag = det_re * det_re + det_im * det_im
    dinv_re, dinv_im = (det_re / det_mag, -det_im / det_mag)
    grav = gravity[None]
    hb_re, hb_im = cmul(b_re, b_im, h0r, h0i)
    zr, zi, dr, di, hr, hi = (z0r, z0i, d0r, d0i, h0r, h0i)
    for sweep in range(SWEEPS):
        if sweep == 0:
            rzr, rzi, rdr, rdi = (z0r, z0i, d0r, d0i)
        else:
            both = jnp.stack([zr, zi, dr, di], axis=0)
            ext = extend(both)
            lower = jnp.stack([ext[:, :, 1, :, 0:count], ext[:, :, 0, :, 1 : count + 1]], axis=2)
            upper = jnp.stack(
                [ext[:, :, 1, :, 1 : count + 1], ext[:, :, 0, :, 2 : count + 2]], axis=2
            )
            near = e_lo * lower + e_hi * upper
            rzr = z0r - coriolis_step * near[2]
            rzi = z0i - coriolis_step * near[3]
            rdr = d0r + coriolis_step * near[0]
            rdi = d0i + coriolis_step * near[1]
        zr, zi = cmul(rzr, rzi, inv_re, inv_im)
        nd_re, nd_im = cmul(shift_re, shift_im, rdr, rdi)
        nd_re = nd_re + grav * h0r
        nd_im = nd_im + grav * h0i
        nh_re = hb_re - grav * rdr
        nh_im = hb_im - grav * rdi
        dr, di = cmul(nd_re, nd_im, dinv_re, dinv_im)
        hr, hi = cmul(nh_re, nh_im, dinv_re, dinv_im)
    parts = []
    for field_re, field_im in ((zr, zi), (dr, di), (hr, hi)):
        out_re, out_im = cmul(weight_re, weight_im, field_re, field_im)
        parts.append(jnp.sum(out_re, axis=0))
        parts.append(jnp.sum(out_im, axis=0))
    return jnp.stack(parts, axis=0)


def lookup(pole_table, chosen):
    columns = jnp.arange(pole_table.shape[1], dtype=jnp.int32)
    onehot = (chosen[:, None] == columns[None, :]).astype(jnp.float32)
    return jnp.dot(onehot, jnp.transpose(pole_table), precision=lax.Precision.HIGHEST)


def shards(grid, legendre, wave_table, pole_table, pole_index):
    slots = legendre.shape[0]
    local_k = legendre.shape[3]
    lat_rows = grid.shape[2]
    wave_count = lax.axis_size("wave")
    half_count = wave_count // 2
    columns = jnp.take(grid, wave_table, axis=1)
    regrouped = lax.all_to_all(columns[None], "wave", split_axis=2, concat_axis=0, tiled=True)
    north = regrouped[:half_count]
    south = regrouped[half_count:]
    parts = jnp.stack([north + south, north - south], axis=0)
    high, low = split_high(parts)
    leg_blocks = legendre.reshape(slots, 2, half_count, lat_rows, local_k)
    first = jnp.einsum("mpwlk,pwcml->cpmk", leg_blocks, high, preferred_element_type=jnp.float32)
    second = jnp.einsum("mpwlk,pwcml->cpmk", leg_blocks, low, preferred_element_type=jnp.float32)
    spectra = first + second
    own_waves = lax.dynamic_slice_in_dim(wave_table, lax.axis_index("wave") * slots, slots).astype(
        jnp.float32
    )
    whole = lax.all_gather(spectra, "pole", axis=3, tiled=True)
    per_device = pole_index.shape[0] // lax.axis_size("pole")
    chosen = lax.dynamic_slice_in_dim(pole_index, lax.axis_index("pole") * per_device, per_device)
    coef = coefficients(own_waves, whole.shape[3])
    partial_terms = solve(whole, coef, lookup(pole_table, chosen), zero_extend)
    result = lax.psum_scatter(partial_terms, "pole", scatter_dimension=3, tiled=True)
    return result


def solution(mesh):
    in_specs = (P(None, None, "wave"), P("wave", None, None, "pole"), P(), P(), P())
    out_specs = P(None, None, "wave", "pole")
    return jax.shard_map(shards, mesh=mesh, in_specs=in_specs, out_specs=out_specs, check_vma=False)
```

profile of v0, /device:TPU:0, one launch (start us, length us, event | category | flops | bytes accessed | tf_op | source)
XLA Modules:
  0.0 192.9 jit_solution(7145403172599582811)
XLA Ops:
  6.5 0.7 compare_and_fusion
  7.2 0.7 compare_select_fusion
  7.9 2.8 %copy.19 = f32[6,256,192]{2,0,1:T(8,128)} copy(f32[6,256,192]{1,2,0:T(8,128)} %param.5) | data formatting | bytes 2359296 | tf_op args[0]
  10.8 2.3 %gather_fusion = f32[256,6,192]{2,1,0:T(8,128)S(1)} fusion(f32[6,256,192]{2,0,1:T(8,128)} %copy.19, s32[1024]{0:T(1024)S(1)} %pad_clamp_fusion), kind=kCustom, calls=%fused_computation | custom fusion | bytes 2360320 | tf_op jit(solution)/shard_map/jit(_take)/gather | solution.py:108
  13.5 2.8 %copy.20 = f32[1,6,256,192]{3,0,1,2:T(1,128)} copy(f32[1,6,256,192]{3,1,2,0:T(8,128)S(1)} %bitcast_select_fusion) | data formatting | bytes 2359296 | tf_op jit(solution)/shard_map/jit(_take)/select_n | solution.py:108
  16.2 6.1 %all-to-all-start = ((f32[1,6,256,192]{3,0,1,2:T(1,128)}), f32[1,6,256,192]{3,0,1,2:T(1,128)S(1)}, u32[]{:S(2)}, u32[]{:S(2)}) async-start(f32[1,6,256,192]{3,0,1,2:T(1,128)} %copy.20), calls=%async_computation | async-start | bytes 3145728 | tf_op jit(solution)/shard_map/all_to_all | solution.py:109
  23.2 21.3 %all-to-all-done = f32[1,6,256,192]{3,0,1,2:T(1,128)S(1)} async-done(((f32[1,6,256,192]{3,0,1,2:T(1,128)}), f32[1,6,256,192]{3,0,1,2:T(1,128)S(1)}, u32[]{:S(2)}, u32[]{:S(2)}) %all-to-all-start) | async-done | bytes 1179680 | tf_op jit(solution)/shard_map/all_to_all | solution.py:109
  44.7 0.9 copy.56
  46.1 6.8 %fusion.12 = f32[2,16,6,128]{3,2,1,0:T(8,128)S(1)} fusion(bf16[2,8,6,16,192]{4,2,1,3,0:T(8,128)(2,1)S(1)} %fusion.11, bf16[16,2,8,192,128]{4,3,2,1,0:T(8,128)(2,1)} %bitcast.123), kind=kOutput, calls=%fused_computation.72 | convolution fusion | flops 75497472 | bytes 13271040 | tf_op jit(solution)/shard_map/mpwlk,pwcml->cpmk/dot_general | solution.py:115
  53.1 2.2 %fusion.21 = f32[6,2,16,128]{3,0,2,1:T(8,128)S(1)} fusion(f32[2,16,6,128]{3,2,1,0:T(8,128)S(1)} %fusion.12, bf16[16,2,8,192,128]{4,3,2,1,0:T(8,128)(2,1)S(1)} %bitcast.126, bf16[2,8,6,16,192]{4,2,1,3,0:T(8,128)(2,1)S(1)} %fusion.11, f32[1,8,6,16,192]{4,2,1,3,0:T(8,128)S(1)} %get-tuple-element.86, f32[1,8,6,16,192]{4,2,1,3,0:T(8,128)S(1)} %get-tuple-element.85), kind=kOutput, calls=%fused_computation.75 | convolution fusion | flops 76701696 | bytes 14548992 | tf_op jit(solution)/shard_map/mpwlk,pwcml->cpmk/dot_general | solution.py:116
  55.2 37.6 %all_gather.3 = f32[6,2,16,1024]{3,0,2,1:T(8,128)S(1)} all-gather(f32[6,2,16,128]{3,0,2,1:T(8,128)S(1)} %fusion.21), channel_id=1, replica_groups=mesh['wave'=16,'pole'=8] {'pole'}, dimensions={3}, use_global_device_ids=true | all-gather | bytes 884736 | tf_op jit(solution)/shard_map/all_gather | solution.py:121
  92.8 0.9 fusion.99
  93.9 0.8 multiply_subtract_fusion.16
  95.0 0.8 fusion.110
  96.3 0.9 multiply_subtract_fusion.14
  97.4 0.8 fusion.109
  98.8 0.9 multiply_subtract_fusion.12
  99.9 0.8 fusion.108
  101.2 0.9 multiply_subtract_fusion.10
  102.4 0.8 fusion.107
  103.7 0.9 multiply_subtract_fusion.8
  104.8 1.0 fusion.106
  105.9 0.5 fusion.8
  106.4 0.9 multiply_subtract_fusion.6
  107.5 0.8 fusion.105
  108.3 0.5 fusion.9
  108.9 0.9 multiply_subtract_fusion.4
  110.0 0.8 fusion.104
  111.8 0.7 multiply_add_fusion
  112.5 1.1 add_reduce_fusion
  113.7 0.9 copy-done.2
  114.6 71.5 %reduce-scatter.2.cloned.1.call-done = f32[6,2,16,128]{3,2,1,0:T(8,128)} async-done(((f32[6,2,16,1024]{3,2,1,0:T(8,128)}), f32[6,2,16,128]{3,2,1,0:T(8,128)}) %reduce-scatter.2.cloned.1.call-update) | async-done | bytes 98320 | tf_op jit(solution)/shard_map/reduce_scatter | solution.py:126
  (55 shorter events, 6.4 us)
Async XLA Ops:
  6.5 16.1 %copy-start = (f32[4,64]{1,0:T(4,128)S(1)}, f32[4,64]{1,0:T(4,128)}, u32[]{:S(2)}) copy-start(f32[4,64]{1,0:T(4,128)} %param.8) | copy-start | bytes 3076
  16.2 6.2 %copy-start.3 = (s32[256]{0:T(256)S(1)}, s32[256]{0:T(256)}, u32[]{:S(2)}) copy-start(s32[256]{0:T(256)} %param.7) | copy-start | bytes 3076
  16.2 6.3 %copy-start.4 = (s32[32]{0:T(128)S(1)}, s32[32]{0:T(128)}, u32[]{:S(2)}) copy-start(s32[32]{0:T(128)} %param.9) | copy-start | bytes 388
  16.2 28.2 %all-to-all-start = ((f32[1,6,256,192]{3,0,1,2:T(1,128)}), f32[1,6,256,192]{3,0,1,2:T(1,128)S(1)}, u32[]{:S(2)}, u32[]{:S(2)}) async-start(f32[1,6,256,192]{3,0,1,2:T(1,128)} %copy.20), calls=%async_computation | async-start | bytes 3145728 | tf_op jit(solution)/shard_map/all_to_all | solution.py:109
  22.4 163.6 %reduce-scatter.2.cloned.1.call-start = ((), (), s32[]{:S(2)}) async-start(), calls=%async_computation.2 | async-start | bytes 884736 | tf_op jit(solution)/shard_map/reduce_scatter | solution.py:126
  44.6 8.3 %slice-start = ((s8[12582912]{0:T(1024)(128)(4,1)}), s8[4194304]{0:T(1024)(128)(4,1)S(1)}, s32[]{:S(2)}) async-start(s8[12582912]{0:T(1024)(128)(4,1)} %bitcast.124), calls=%async_computation.3 | async-start | bytes 8388608
  45.8 7.1 %slice-start.1 = ((s8[12582912]{0:T(1024)(128)(4,1)}), s8[4194304]{0:T(1024)(128)(4,1)S(1)}, s32[]{:S(2)}) async-start(s8[12582912]{0:T(1024)(128)(4,1)} %bitcast.124), calls=%async_computation.4 | async-start | bytes 8388608
  46.1 6.9 %slice-start.2 = ((s8[12582912]{0:T(1024)(128)(4,1)}), s8[4194304]{0:T(1024)(128)(4,1)S(1)}, s32[]{:S(2)}) async-start(s8[12582912]{0:T(1024)(128)(4,1)} %bitcast.124), calls=%async_computation.5 | async-start | bytes 8388608
  112.5 73.6 %copy-start.1 = (f32[4,64]{1,0:T(4,128)S(1)}, f32[4,64]{1,0:T(4,128)}, u32[]{:S(2)}) copy-start(f32[4,64]{1,0:T(4,128)} %param.8) | copy-start | bytes 3076
  113.7 0.9 copy-start.2
Sparse Core Ops, SparseCore 0:
  114.7 71.3 reduce-scatter.1
where the time goes:
time: 193 us
  waiting for transfers between devices  92.8 us (48%)
  blocking collectives  37.6 us (19%)
  other arithmetic  17 us (9%)
  local copies, waits for them, and re-layouts  16.4 us (8%)
  between operations  13.8 us (7%)
  matrix products  9.14 us (5%)
  starting transfers between devices  6.18 us (3%)
    reduce_scatter x1, waiting for transfers between devices, shards(): lax.psum_scatter(partial_terms, 'pole', scatter_dimension=3, tiled=True)  71.5 us
    all_gather x1, blocking collectives, shards(): whole = lax.all_gather(spectra, 'pole', axis=3, tiled=True)  37.6 us
    all_to_all x1, waiting for transfers between devices, shards(): lax.all_to_all(columns[None], 'wave', split_axis=2, concat_axis=0, tiled=...  21.3 us
    dot_general x1, matrix products, shards(): jnp.einsum('mpwlk,pwcml->cpmk', leg_blocks, high, preferred_element_type=...  6.8 us
    sub x8, other arithmetic, cmul(): return (are * bre - aim * bim, are * bim + aim * bre)  6.75 us
    all_to_all x1, starting transfers between devices, shards(): lax.all_to_all(columns[None], 'wave', split_axis=2, concat_axis=0, tiled=...  6.14 us
    slice x7, local copies, waits for them, and re-layouts, solve(): ext[:, :, 1, :, 1:count + 1]  5.96 us
    unnamed x26, local copies, waits for them, and re-layouts  4.13 us
  transfers between devices with their start and end apart: 2, of which 2 were waited for; matrix products, arithmetic and copies ran while one was open for 0% of the time, Pallas kernels for 0%

commit v1 on v0

--- a/solution.py
+++ b/solution.py
@@ -118,7 +118,9 @@
     own_waves = lax.dynamic_slice_in_dim(wave_table, lax.axis_index("wave") * slots, slots).astype(
         jnp.float32
     )
-    whole = lax.all_gather(spectra, "pole", axis=3, tiled=True)
+    whole = jnp.concatenate(
+        lax.all_to_all(jnp.stack([spectra] * lax.axis_size("pole")), "pole", 0, 0), axis=3
+    )
     per_device = pole_index.shape[0] // lax.axis_size("pole")
     chosen = lax.dynamic_slice_in_dim(pole_index, lax.axis_index("pole") * per_device, per_device)
     coef = coefficients(own_waves, whole.shape[3])

time: 193 us -> 175 us (0.907)
  blocking collectives: 37.6 us -> 0 us
  waiting for transfers between devices: 92.8 us -> 104 us
  starting transfers between devices: 6.18 us -> 13.7 us
    all_gather x1 -> x0, blocking collectives: 37.6 us -> none  [shards(): whole = lax.all_gather(spectra, 'pole', axis=3, tiled=True)]
    all_to_all x0 -> x1, waiting for transfers between devices: none -> 12.5 us  [shards(): lax.all_to_all(jnp.stack([spectra] * lax.axis_size('pole')), 'pole', 0, 0)]
    all_to_all x0 -> x1, starting transfers between devices: none -> 7.32 us  [shards(): lax.all_to_all(jnp.stack([spectra] * lax.axis_size('pole')), 'pole', 0, 0)]
    unnamed x26 -> x22, local copies, waits for them, and re-layouts: 4.13 us -> 3.93 us
  transfers between devices with their start and end apart: 2 -> 3, of which waited for: 2 -> 3; matrix products, arithmetic and copies ran while one was open for 0% -> 0% of each run, Pallas kernels for 0% -> 0%
where the time goes in v1:
time: 175 us
  waiting for transfers between devices  104 us (59%)
  local copies, waits for them, and re-layouts  17.7 us (10%)
  other arithmetic  16.4 us (9%)
  between operations  13.9 us (8%)
  starting transfers between devices  13.7 us (8%)
  matrix products  9.14 us (5%)
    reduce_scatter x1, waiting for transfers between devices, shards(): lax.psum_scatter(partial_terms, 'pole', scatter_dimension=3, tiled=True)  69.8 us
    all_to_all x1, waiting for transfers between devices, shards(): lax.all_to_all(columns[None], 'wave', split_axis=2, concat_axis=0, tiled=...  22 us
    all_to_all x1, waiting for transfers between devices, shards(): lax.all_to_all(jnp.stack([spectra] * lax.axis_size('pole')), 'pole', 0, 0)  12.5 us
    all_to_all x1, starting transfers between devices, shards(): lax.all_to_all(jnp.stack([spectra] * lax.axis_size('pole')), 'pole', 0, 0)  7.32 us
    dot_general x1, matrix products, shards(): jnp.einsum('mpwlk,pwcml->cpmk', leg_blocks, high, preferred_element_type=...  6.8 us
    sub x8, other arithmetic, cmul(): return (are * bre - aim * bim, are * bim + aim * bre)  6.75 us
    all_to_all x1, starting transfers between devices, shards(): lax.all_to_all(columns[None], 'wave', split_axis=2, concat_axis=0, tiled=...  6.14 us
    slice x7, local copies, waits for them, and re-layouts, solve(): ext[:, :, 1, :, 1:count + 1]  5.75 us
  transfers between devices with their start and end apart: 3, of which 3 were waited for; matrix products, arithmetic and copies ran while one was open for 0% of the time, Pallas kernels for 0%

profile of v1, /device:TPU:0, one launch (start us, length us, event | category | flops | bytes accessed | tf_op | source)
XLA Modules:
  0.0 175.1 jit_solution(3673953221735133096)
XLA Ops:
  6.5 0.7 compare_and_fusion
  7.2 0.7 compare_select_fusion
  7.9 2.8 %copy.35 = f32[6,256,192]{2,0,1:T(8,128)} copy(f32[6,256,192]{1,2,0:T(8,128)} %param.5) | data formatting | bytes 2359296 | tf_op args[0]
  10.8 2.3 %gather_fusion = f32[256,6,192]{2,1,0:T(8,128)S(1)} fusion(f32[6,256,192]{2,0,1:T(8,128)} %copy.35, s32[1024]{0:T(1024)S(1)} %pad_clamp_fusion), kind=kCustom, calls=%fused_computation | custom fusion | bytes 2360320 | tf_op jit(solution)/shard_map/jit(_take)/gather | solution.py:108
  13.5 2.8 %copy.36 = f32[1,6,256,192]{3,0,1,2:T(1,128)} copy(f32[1,6,256,192]{3,1,2,0:T(8,128)S(1)} %bitcast_select_fusion) | data formatting | bytes 2359296 | tf_op jit(solution)/shard_map/jit(_take)/select_n | solution.py:108
  16.3 6.1 %all-to-all-start = ((f32[1,6,256,192]{3,0,1,2:T(1,128)}), f32[1,6,256,192]{3,0,1,2:T(1,128)S(1)}, u32[]{:S(2)}, u32[]{:S(2)}) async-start(f32[1,6,256,192]{3,0,1,2:T(1,128)} %copy.36), calls=%async_computation | async-start | bytes 3145728 | tf_op jit(solution)/shard_map/all_to_all | solution.py:109
  22.5 22.0 %all-to-all-done = f32[1,6,256,192]{3,0,1,2:T(1,128)S(1)} async-done(((f32[1,6,256,192]{3,0,1,2:T(1,128)}), f32[1,6,256,192]{3,0,1,2:T(1,128)S(1)}, u32[]{:S(2)}, u32[]{:S(2)}) %all-to-all-start) | async-done | bytes 1179680 | tf_op jit(solution)/shard_map/all_to_all | solution.py:109
  44.7 0.9 copy.63
  46.1 6.8 %fusion.12 = f32[2,16,6,128]{3,2,1,0:T(8,128)S(1)} fusion(bf16[2,8,6,16,192]{4,2,1,3,0:T(8,128)(2,1)S(1)} %fusion.11, bf16[16,2,8,192,128]{4,3,2,1,0:T(8,128)(2,1)} %bitcast.120), kind=kOutput, calls=%fused_computation.72 | convolution fusion | flops 75497472 | bytes 13271040 | tf_op jit(solution)/shard_map/mpwlk,pwcml->cpmk/dot_general | solution.py:115
  53.1 2.2 %fusion.21 = f32[6,2,16,128]{3,0,2,1:T(8,128)S(1)} fusion(f32[2,16,6,128]{3,2,1,0:T(8,128)S(1)} %fusion.12, bf16[16,2,8,192,128]{4,3,2,1,0:T(8,128)(2,1)S(1)} %bitcast.123, bf16[2,8,6,16,192]{4,2,1,3,0:T(8,128)(2,1)S(1)} %fusion.11, f32[1,8,6,16,192]{4,2,1,3,0:T(8,128)S(1)} %get-tuple-element.86, f32[1,8,6,16,192]{4,2,1,3,0:T(8,128)S(1)} %get-tuple-element.85), kind=kOutput, calls=%fused_computation.75 | convolution fusion | flops 76701696 | bytes 14548992 | tf_op jit(solution)/shard_map/mpwlk,pwcml->cpmk/dot_general | solution.py:116
  55.3 1.0 stack.61
  56.2 7.3 %all-to-all-start.1 = ((f32[8,6,2,16,128]{4,3,2,1,0:T(8,128)}), f32[8,6,2,16,128]{4,3,2,1,0:T(8,128)S(1)}, u32[]{:S(2)}, u32[]{:S(2)}) async-start(f32[8,6,2,16,128]{4,3,2,1,0:T(8,128)} %stack.61), calls=%async_computation.1 | async-start | bytes 1572864 | tf_op jit(solution)/shard_map/all_to_all | solution.py:122
  64.2 12.5 %all-to-all-done.1 = f32[8,6,2,16,128]{4,3,2,1,0:T(8,128)S(1)} async-done(((f32[8,6,2,16,128]{4,3,2,1,0:T(8,128)}), f32[8,6,2,16,128]{4,3,2,1,0:T(8,128)S(1)}, u32[]{:S(2)}, u32[]{:S(2)}) %all-to-all-start.1) | async-done | bytes 786464 | tf_op jit(solution)/shard_map/all_to_all | solution.py:122
  77.8 0.8 multiply_subtract_fusion.16
  78.8 0.8 fusion.108
  80.2 0.9 multiply_subtract_fusion.14
  81.3 0.8 fusion.107
  82.7 0.9 multiply_subtract_fusion.12
  83.8 0.8 fusion.106
  85.2 0.9 multiply_subtract_fusion.10
  86.3 0.8 fusion.105
  87.7 0.9 multiply_subtract_fusion.8
  88.8 0.8 fusion.104
  89.6 0.7 fusion.8
  90.3 0.9 multiply_subtract_fusion.6
  91.5 0.8 fusion.103
  92.8 0.9 multiply_subtract_fusion.4
  93.9 0.8 fusion.102
  95.7 0.7 multiply_add_fusion
  96.4 1.1 add_reduce_fusion
  97.6 0.9 copy-done.2
  98.5 69.8 %reduce-scatter.2.cloned.1.call-done = f32[6,2,16,128]{3,2,1,0:T(8,128)} async-done(((f32[6,2,16,1024]{3,2,1,0:T(8,128)}), f32[6,2,16,128]{3,2,1,0:T(8,128)}) %reduce-scatter.2.cloned.1.call-update) | async-done | bytes 98320 | tf_op jit(solution)/shard_map/reduce_scatter | solution.py:128
  (66 shorter events, 7.7 us)
Async XLA Ops:
  6.5 57.4 %copy-start = (f32[4,64]{1,0:T(4,128)S(1)}, f32[4,64]{1,0:T(4,128)}, u32[]{:S(2)}) copy-start(f32[4,64]{1,0:T(4,128)} %param.8) | copy-start | bytes 3076
  16.3 6.2 %copy-start.3 = (s32[256]{0:T(256)S(1)}, s32[256]{0:T(256)}, u32[]{:S(2)}) copy-start(s32[256]{0:T(256)} %param.7) | copy-start | bytes 3076
  16.3 28.2 %all-to-all-start = ((f32[1,6,256,192]{3,0,1,2:T(1,128)}), f32[1,6,256,192]{3,0,1,2:T(1,128)S(1)}, u32[]{:S(2)}, u32[]{:S(2)}) async-start(f32[1,6,256,192]{3,0,1,2:T(1,128)} %copy.36), calls=%async_computation | async-start | bytes 3145728 | tf_op jit(solution)/shard_map/all_to_all | solution.py:109
  44.7 8.3 %slice-start = ((s8[12582912]{0:T(1024)(128)(4,1)}), s8[4194304]{0:T(1024)(128)(4,1)S(1)}, s32[]{:S(2)}) async-start(s8[12582912]{0:T(1024)(128)(4,1)} %bitcast.121), calls=%async_computation.4 | async-start | bytes 8388608
  45.9 7.1 %slice-start.1 = ((s8[12582912]{0:T(1024)(128)(4,1)}), s8[4194304]{0:T(1024)(128)(4,1)S(1)}, s32[]{:S(2)}) async-start(s8[12582912]{0:T(1024)(128)(4,1)} %bitcast.121), calls=%async_computation.5 | async-start | bytes 8388608
  46.1 6.9 %slice-start.2 = ((s8[12582912]{0:T(1024)(128)(4,1)}), s8[4194304]{0:T(1024)(128)(4,1)S(1)}, s32[]{:S(2)}) async-start(s8[12582912]{0:T(1024)(128)(4,1)} %bitcast.121), calls=%async_computation.6 | async-start | bytes 8388608
  55.2 8.6 %copy-start.4 = (s32[32]{0:T(128)S(1)}, s32[32]{0:T(128)}, u32[]{:S(2)}) copy-start(s32[32]{0:T(128)} %param.9) | copy-start | bytes 388
  56.2 20.5 %all-to-all-start.1 = ((f32[8,6,2,16,128]{4,3,2,1,0:T(8,128)}), f32[8,6,2,16,128]{4,3,2,1,0:T(8,128)S(1)}, u32[]{:S(2)}, u32[]{:S(2)}) async-start(f32[8,6,2,16,128]{4,3,2,1,0:T(8,128)} %stack.61), calls=%async_computation.1 | async-start | bytes 1572864 | tf_op jit(solution)/shard_map/all_to_all | solution.py:122
  63.6 104.7 %reduce-scatter.2.cloned.1.call-start = ((), (), s32[]{:S(2)}) async-start(), calls=%async_computation.3 | async-start | bytes 884736 | tf_op jit(solution)/shard_map/reduce_scatter | solution.py:128
  96.4 71.9 %copy-start.1 = (f32[4,64]{1,0:T(4,128)S(1)}, f32[4,64]{1,0:T(4,128)}, u32[]{:S(2)}) copy-start(f32[4,64]{1,0:T(4,128)} %param.8) | copy-start | bytes 3076
  97.6 0.9 copy-start.2
Sparse Core Ops, SparseCore 0:
  98.6 69.6 reduce-scatter.1
